TPU v7x, 512 devices: a whole 4x4x16 slice. The times are simulated.
512 devices in a mesh: seq: 32 (over z, core), tensor: 16 (over y, x).
Axes of the slice: x: 4, y: 4, z: 16, core: 2. Of those that a mesh axis runs over, the one named last changes fastest.
Arguments:
- hidden: bfloat16 [4, 64, 5120], P(None, None, 'seq'), may hold values from -400 to 400
- norm_gain: bfloat16 [5120], P('seq'), may hold values from 0.099609375 to 1.8984375
- w_qkv: bfloat16 [5120, 7168], P('seq', 'tensor'), may hold values from -0.078125 to 0.078125
- b_qkv: bfloat16 [7168], P('tensor'), may hold values from -3 to 3
- w_out: bfloat16 [5120, 5120], P('tensor', 'seq'), may hold values from -0.078125 to 0.078125
- prefix_key_cache: bfloat16 [16, 12288, 1024], P('tensor', 'seq'), may hold values from -140 to 140
- prefix_value_cache: bfloat16 [16, 12288, 1024], P('tensor', 'seq'), may hold values from -6 to 6
- suffix_key_cache: bfloat16 [64, 4096, 1024], P('tensor', 'seq'), may hold values from -8 to 8
- suffix_value_cache: bfloat16 [64, 4096, 1024], P('tensor', 'seq'), may hold values from -6 to 6
- prefix_lens: int32 [16], P('tensor'), may hold values from 1 to 12288, as said below
- suffix_lens: int32 [64], P('tensor'), may hold values from 0 to 4096, as said below
Outputs:
- attn_out: float32 [4, 64, 5120], P(None, 'tensor', 'seq')
- new_keys: float32 [64, 4, 1024], P('tensor')
- new_values: float32 [64, 4, 1024], P('tensor')
Inputs may be any that keep to these rules, and one draw needn't show every extreme that they name: `prefix_lens`: some group has exactly 12288 live slots and some exactly one. `suffix_lens`: some request has exactly 4096 live slots and some none.
All inputs are finite; a program needn't handle non-finite values.
Results may differ from a plain program's by a relative error of at most 0.012.
The roundings to bfloat16 on the way count: a program that leaves them out, or rounds other values in their place, can miss the bound.
Values may be sent and summed in bfloat16 or wider, within the bound.
No kernel may reach another device: no remote copies, remote signals or barrier semaphores. Data moves between devices by JAX's collectives and lax.ppermute only.
A program may use at most 64 MiB of HBM per device.

v0:
```python
import jax
import jax.numpy as jnp
from jax import lax
from jax.sharding import PartitionSpec as P

D = 5120
QUERY_HEADS = 40
KEY_HEADS = 8
HEAD_SIZE = 128
KEY_COLUMNS = 1024
epsilon = 1e-06
masked_fill = -1e30


def apply_rotary(values, token_positions):
    half = values.shape[-1] // 2
    freq = jnp.exp(
        -(jnp.arange(half, dtype=jnp.float32) * (2.0 / values.shape[-1]))
        * jnp.log(jnp.float32(1000000.0))
    )
    angles = token_positions[..., None, None] * freq
    cosine = jnp.cos(angles)
    sine = jnp.sin(angles)
    left = values[..., :half]
    right = values[..., half:]
    return jnp.concatenate([left * cosine - right * sine, right * cosine + left * sine], axis=-1)


def body(
    hidden,
    norm_gain,
    w_qkv,
    b_qkv,
    w_out,
    prefix_key_cache,
    prefix_value_cache,
    suffix_key_cache,
    suffix_value_cache,
    prefix_lens,
    suffix_lens,
):
    decode_step_count = hidden.shape[0]
    request_count = suffix_lens.shape[0]
    prefix_count = prefix_key_cache.shape[1]
    suffix_count = suffix_key_cache.shape[1]
    query_group_width = QUERY_HEADS // KEY_HEADS
    query_width = QUERY_HEADS * HEAD_SIZE
    query_rows = decode_step_count * query_group_width
    scale = float(HEAD_SIZE) ** (-0.5)
    seq_index = lax.axis_index("seq")
    xf = hidden.astype(jnp.float32)
    squares = lax.psum(jnp.sum(xf * xf, axis=2), "seq")
    normed = (
        xf * lax.rsqrt(squares / D + epsilon)[..., None] * norm_gain.astype(jnp.float32)
    ).astype(jnp.bfloat16)
    partial_value = jnp.einsum("sbd,dc->sbc", normed, w_qkv, preferred_element_type=jnp.float32)
    bias = b_qkv.astype(jnp.float32)
    summed_cols = lax.psum(partial_value, "seq") + bias
    combined_output = lax.all_to_all(summed_cols, "tensor", split_axis=1, concat_axis=2, tiled=True)
    token_positions = (
        (prefix_lens[0] + suffix_lens)[None, :]
        + jnp.arange(decode_step_count, dtype=jnp.int32)[:, None]
    ).astype(jnp.float32)
    query_matrix = apply_rotary(
        combined_output[..., :query_width].reshape(
            decode_step_count, request_count, QUERY_HEADS, HEAD_SIZE
        ),
        token_positions,
    ).astype(jnp.bfloat16)
    keys_float = apply_rotary(
        combined_output[..., query_width : query_width + KEY_COLUMNS].reshape(
            decode_step_count, request_count, KEY_HEADS, HEAD_SIZE
        ),
        token_positions,
    )
    values_float = combined_output[..., query_width + KEY_COLUMNS :].reshape(
        decode_step_count, request_count, KEY_HEADS, HEAD_SIZE
    )
    current_keys = keys_float.astype(jnp.bfloat16)
    current_values = values_float.astype(jnp.bfloat16)
    new_keys = keys_float.reshape(decode_step_count, request_count, KEY_COLUMNS).transpose(1, 0, 2)
    new_values = values_float.reshape(decode_step_count, request_count, KEY_COLUMNS).transpose(
        1, 0, 2
    )
    query_by_group = (
        query_matrix.reshape(
            decode_step_count, request_count, KEY_HEADS, query_group_width, HEAD_SIZE
        )
        .transpose(1, 2, 0, 3, 4)
        .reshape(request_count, KEY_HEADS, query_rows, HEAD_SIZE)
    )
    prefix_key_block = prefix_key_cache[0].reshape(prefix_count, KEY_HEADS, HEAD_SIZE)
    prefix_value_block = prefix_value_cache[0].reshape(prefix_count, KEY_HEADS, HEAD_SIZE)
    suffix_key_block = suffix_key_cache.reshape(request_count, suffix_count, KEY_HEADS, HEAD_SIZE)
    suffix_value_block = suffix_value_cache.reshape(
        request_count, suffix_count, KEY_HEADS, HEAD_SIZE
    )
    score_pre = (
        jnp.einsum(
            "rhqd,phd->rhqp", query_by_group, prefix_key_block, preferred_element_type=jnp.float32
        )
        * scale
    )
    score_suf = (
        jnp.einsum(
            "rhqd,rshd->rhqs", query_by_group, suffix_key_block, preferred_element_type=jnp.float32
        )
        * scale
    )
    pre_mask = (
        seq_index * prefix_count + jnp.arange(prefix_count, dtype=jnp.int32) < prefix_lens[0]
    )[None, None, None, :]
    suf_mask = (
        (seq_index * suffix_count + jnp.arange(suffix_count, dtype=jnp.int32))[None, :]
        < suffix_lens[:, None]
    )[:, None, None, :]
    fill_pre = jnp.where(pre_mask, score_pre, masked_fill)
    fill_suf = jnp.where(suf_mask, score_suf, masked_fill)
    local_max = jnp.maximum(jnp.max(fill_pre, axis=3), jnp.max(fill_suf, axis=3))
    prob_pre = jnp.where(pre_mask, jnp.exp(fill_pre - local_max[..., None]), 0.0)
    prob_suf = jnp.where(suf_mask, jnp.exp(fill_suf - local_max[..., None]), 0.0)
    local_weight = jnp.sum(prob_pre, axis=3) + jnp.sum(prob_suf, axis=3)
    local_acc = jnp.einsum(
        "rhqp,phd->rhqd",
        prob_pre.astype(jnp.bfloat16),
        prefix_value_block,
        preferred_element_type=jnp.float32,
    )
    local_acc = local_acc + jnp.einsum(
        "rhqs,rshd->rhqd",
        prob_suf.astype(jnp.bfloat16),
        suffix_value_block,
        preferred_element_type=jnp.float32,
    )
    global_max = lax.pmax(local_max, "seq")
    factor = jnp.exp(local_max - global_max)
    global_weight, global_acc = lax.psum(
        (local_weight * factor, local_acc * factor[..., None]), "seq"
    )
    fresh_k = current_keys.transpose(1, 2, 0, 3)
    fresh_v = current_values.transpose(1, 2, 0, 3)
    score_new = (
        jnp.einsum("rhqd,rhid->rhqi", query_by_group, fresh_k, preferred_element_type=jnp.float32)
        * scale
    )
    new_mask = (
        (jnp.arange(query_rows, dtype=jnp.int32) // query_group_width)[:, None]
        >= jnp.arange(decode_step_count, dtype=jnp.int32)[None, :]
    )[None, None]
    fill_new = jnp.where(new_mask, score_new, masked_fill)
    new_max = jnp.max(fill_new, axis=3)
    prob_new = jnp.where(new_mask, jnp.exp(fill_new - new_max[..., None]), 0.0)
    top = jnp.maximum(global_max, new_max)
    factor_old = jnp.exp(global_max - top)
    factor_new = jnp.exp(new_max - top)
    total = global_weight * factor_old + jnp.sum(prob_new, axis=3) * factor_new
    new_acc = jnp.einsum(
        "rhqi,rhid->rhqd",
        prob_new.astype(jnp.bfloat16),
        fresh_v,
        preferred_element_type=jnp.float32,
    )
    summed = global_acc * factor_old[..., None] + new_acc * factor_new[..., None]
    attention_output = (summed / total[..., None]).astype(jnp.bfloat16)
    heads_local = (
        attention_output.reshape(
            request_count, KEY_HEADS, decode_step_count, query_group_width, HEAD_SIZE
        )
        .transpose(2, 0, 1, 3, 4)
        .reshape(decode_step_count, request_count, query_width)
    )
    by_heads = lax.all_to_all(heads_local, "tensor", split_axis=2, concat_axis=1, tiled=True)
    projected = jnp.einsum("sbc,cd->sbd", by_heads, w_out, preferred_element_type=jnp.float32)
    owned = lax.psum_scatter(projected, "tensor", scatter_dimension=1, tiled=True)
    return (owned, new_keys, new_values)


def solution(mesh):
    placed = (
        P(None, None, "seq"),
        P("seq"),
        P("seq", "tensor"),
        P("tensor"),
        P("tensor", "seq"),
        P("tensor", "seq", None),
        P("tensor", "seq", None),
        P("tensor", "seq", None),
        P("tensor", "seq", None),
        P("tensor"),
        P("tensor"),
    )
    return jax.shard_map(
        body,
        mesh=mesh,
        in_specs=placed,
        out_specs=(P(None, "tensor", "seq"), P("tensor", None, None), P("tensor", None, None)),
        check_vma=False,
    )
```

profile of v0, /device:TPU:2, one launch (start us, length us, event | category | flops | bytes accessed | tf_op | source)
XLA Modules:
  0.0 850.0 jit_solution(4505224170774639408)
XLA Ops:
  7.2 0.0 copy-start
  7.2 0.0 copy-start.19
  7.2 0.0 copy-start.16
  7.2 0.0 all-reduce.5.cloned.1.call-start
  7.3 0.8 convert_element_type.43
  8.0 1.0 fusion.22
  9.1 54.7 %psum.28 = f32[4,64]{1,0:T(4,128)S(1)} all-reduce(f32[4,64]{1,0:T(4,128)S(1)} %fusion.22), channel_id=1, replica_groups=mesh['seq'=32,'tensor'=16] {'seq'}, use_global_device_ids=true, to_apply=%region_1.0 | all-reduce | flops 256 | bytes 2048 | tf_op jit(solution)/shard_map/psum | solution.py:52
  63.8 2.1 fusion.29
  65.9 0.0 all-reduce.5.cloned.1.call-update
  66.6 0.1 add_convert_fusion.1
  66.6 0.1 multiply_cosine_fusion
  66.9 0.0 copy-done.4
  66.9 0.2 copy.148
  67.1 2.2 copy.149
  69.3 0.0 copy-done.13
  69.3 199.9 %all-reduce.5.cloned.1.call-done = f32[4,64,448]{2,1,0:T(8,128)} async-done(((f32[4,64,448]{2,1,0:T(8,128)}), f32[4,64,448]{2,1,0:T(8,128)}) %all-reduce.5.cloned.1.call-update) | async-done | bytes 458768 | tf_op jit(solution)/shard_map/psum | solution.py:58
  269.2 1.1 broadcast_add_fusion
  270.4 1.1 copy.98
  271.5 7.3 all-to-all-start
  278.8 0.0 all-reduce.7.cloned.1.call-start
  278.8 0.5 iota_compare_fusion
  279.4 0.1 broadcast_compare_fusion
  279.4 9.8 %all-to-all-done = f32[4,64,448]{2,0,1:T(4,128)S(1)} async-done(((f32[4,64,448]{2,0,1:T(4,128)}), f32[4,64,448]{2,0,1:T(4,128)S(1)}, u32[]{:S(2)}, u32[]{:S(2)}) %all-to-all-start) | async-done | bytes 458784 | tf_op jit(solution)/shard_map/all_to_all | solution.py:59
  289.2 0.3 copy.99
  289.5 0.3 all_to_all.29
  289.9 0.6 slice_bitcast_fusion.1
  290.6 0.1 reshape.150
  290.7 0.2 fusion.51
  290.9 0.4 subtract_convert_fusion
  291.3 0.2 maximum_bitcast_fusion
  291.6 1.4 fusion.52
  293.0 0.7 fusion.53
  293.7 0.0 copy-done.2
  293.7 91.2 %pmax.7 = f32[4,8,20]{2,1,0:T(8,128)} all-reduce(f32[4,8,20]{2,1,0:T(8,128)S(1)} %copy_maximum_fusion), channel_id=1, replica_groups=mesh['seq'=32,'tensor'=16] {'seq'}, use_global_device_ids=true, to_apply=%region_5.6 | all-reduce | flops 640 | bytes 5120 | tf_op jit(solution)/shard_map/pmax | solution.py:135
  384.9 1.5 multiply_subtract_fusion
  386.4 1.9 fusion.20
  388.2 1.1 fusion.12
  389.3 90.0 %psum.31 = f32[4,8,20]{2,1,0:T(8,128)S(1)} all-reduce(f32[4,8,20]{2,1,0:T(8,128)S(1)} %get-tuple-element.6), channel_id=1, replica_groups=mesh['seq'=32,'tensor'=16] {'seq'}, use_global_device_ids=true, to_apply=%region_10.11 | all-reduce | flops 640 | bytes 5120 | tf_op jit(solution)/shard_map/psum | solution.py:137
  479.4 1.3 convolution_bitcast_fusion
  480.7 0.0 copy-done.1
  480.7 0.0 copy-done.6
  480.7 0.0 copy-start.3
  480.7 0.0 copy-start.7
  480.8 1.2 fusion.4
  481.9 0.0 all-reduce.7.cloned.1.call-update
  481.9 0.0 all-reduce.9.cloned.1.call-start
  482.0 0.3 fusion.54
  482.3 0.1 fusion.37
  482.5 198.4 %all-reduce.7.cloned.1.call-done = f32[4,8,20,128]{3,2,0,1:T(8,128)} async-done(((f32[4,8,20,128]{3,2,0,1:T(8,128)}), f32[4,8,20,128]{3,2,0,1:T(8,128)}) %all-reduce.7.cloned.1.call-update) | async-done | bytes 327696 | tf_op jit(solution)/shard_map/psum | solution.py:137
  680.9 1.5 fusion.6
  682.3 0.1 copy.121
  682.4 4.5 copy.139
  686.9 11.0 %reshape.165 = bf16[16,2,2560]{2,1,0:T(2,128)(2,1)S(1)} reshape(bf16[5120,4,4]{2,1,0:T(4,128)(2,1)} %bitcast.84) | data formatting | bytes 327680
  697.9 13.9 %all_to_all.36 = bf16[16,2,2560]{2,1,0:T(2,128)(2,1)S(1)} all-to-all(bf16[16,2,2560]{2,1,0:T(2,128)(2,1)S(1)} %reshape.165), channel_id=1, replica_groups=mesh['seq'=32,'tensor'=16] {'tensor'}, dimensions={0} | all-to-all | bytes 327680 | tf_op jit(solution)/shard_map/all_to_all | solution.py:172
  711.8 12.3 %reshape.166 = bf16[5120,4,4]{2,1,0:T(4,128)(2,1)} reshape(bf16[16,2,2560]{2,1,0:T(2,128)(2,1)S(1)} %all_to_all.36) | data formatting | bytes 327680
  724.1 6.4 copy.140
  730.5 0.1 copy.125
  730.6 0.1 all_to_all.33
  730.7 0.9 fusion.34
  731.7 0.0 all-reduce.9.cloned.1.call-update
  731.7 1.3 dynamic-slice
  733.6 0.7 fusion.46
  734.4 107.7 %all-reduce.9.cloned.1.call-done = f32[4,64,160]{2,1,0:T(8,128)} async-done(((f32[4,64,160]{2,1,0:T(8,128)}), f32[4,64,160]{2,1,0:T(8,128)}) %all-reduce.9.cloned.1.call-update) | async-done | bytes 163856
  842.1 1.4 constant_dynamic-slice_fusion
  (49 shorter events, 0.2 us)
Async XLA Ops:
  7.2 284.4 %copy-start = (bf16[4,128,1024]{2,1,0:T(8,128)(2,1)S(1)}, bf16[4,128,1024]{2,1,0:T(8,128)(2,1)}, u32[]{:S(2)}) copy-start(bf16[4,128,1024]{2,1,0:T(8,128)(2,1)} %param.18) | copy-start | bytes 3145732
  7.2 59.4 %copy-start.19 = (s32[4]{0:T(128)S(1)}, s32[4]{0:T(128)}, u32[]{:S(2)}) copy-start(s32[4]{0:T(128)} %param.21) | copy-start | bytes 52
  7.2 59.6 %copy-start.16 = (bf16[448]{0:T(512)(128)(2,1)S(1)}, bf16[448]{0:T(512)(128)(2,1)}, u32[]{:S(2)}) copy-start(bf16[448]{0:T(512)(128)(2,1)} %param.14) | copy-start | bytes 2692
  7.2 59.7 %copy-start.4 = (bf16[1,384,1024]{2,1,0:T(8,128)(2,1)S(1)}, bf16[1,384,1024]{2,1,0:T(8,128)(2,1)}, u32[]{:S(2)}) copy-start(bf16[1,384,1024]{2,1,0:T(8,128)(2,1)} %param.16) | copy-start | bytes 2359300
  7.2 262.0 %all-reduce.5.cloned.1.call-start = ((), (), s32[]{:S(2)}) async-start(), calls=%async_computation.2 | async-start | bytes 1048576 | tf_op jit(solution)/shard_map/psum | solution.py:58
  66.8 2.5 copy-start.12
  66.8 2.5 copy-start.13
  69.3 223.7 %copy-start.15 = (pred[384]{0:T(512)(128)(4,1)}, pred[384]{0:T(512)(128)(4,1)S(1)}, u32[]{:S(2)}) copy-start(pred[384]{0:T(512)(128)(4,1)S(1)} %add_compare_fusion) | copy-start | bytes 1156
  271.5 17.7 %all-to-all-start = ((f32[4,64,448]{2,0,1:T(4,128)}), f32[4,64,448]{2,0,1:T(4,128)S(1)}, u32[]{:S(2)}, u32[]{:S(2)}) async-start(f32[4,64,448]{2,0,1:T(4,128)} %copy.98), calls=%async_computation | async-start | bytes 1048576 | tf_op jit(solution)/shard_map/all_to_all | solution.py:59
  278.8 402.1 %all-reduce.7.cloned.1.call-start = ((), (), s32[]{:S(2)}) async-start(), calls=%async_computation.3 | async-start | bytes 786432 | tf_op jit(solution)/shard_map/psum | solution.py:137
  279.4 12.2 %copy-start.18 = (pred[4,128]{1,0:T(4,128)(4,1)}, pred[4,128]{1,0:T(4,128)(4,1)S(1)}, u32[]{:S(2)}) copy-start(pred[4,128]{1,0:T(4,128)(4,1)S(1)} %broadcast_compare_fusion) | copy-start | bytes 1540
  291.6 2.1 copy-start.2
  293.7 185.6 %copy-start.5 = (bf16[48,8,8,128]{3,2,1,0:T(8,128)(2,1)S(1)}, bf16[48,8,8,128]{3,2,1,0:T(8,128)(2,1)}, u32[]{:S(2)}) copy-start(bf16[48,8,8,128]{3,2,1,0:T(8,128)(2,1)} %copy.149) | copy-start | bytes 2359300
  384.9 4.4 copy-start.9
  384.9 4.4 copy-start.14
  479.4 1.3 copy-start.1
  479.4 1.3 copy-start.6
  480.7 1.3 copy-start.3
  480.7 1.3 copy-start.7
  480.7 1.3 copy-start.8
  480.7 1.3 copy-start.17
  480.7 1.7 copy-start.10
  481.9 360.1 %all-reduce.9.cloned.1.call-start = ((), (), s32[]{:S(2)}) async-start(), calls=%async_computation.4 | async-start | bytes 524288
  724.1 6.6 copy-start.11
Sparse Core Ops, SparseCore 0:
  66.0 203.1 all-reduce.4
  482.1 198.7 all-reduce.6
  731.8 110.2 all-reduce.8
where the time goes:
time: 851 us; the launch traced here: 850 us
  waiting for transfers between devices  516 us (61%)
  blocking collectives  250 us (29%)
  local copies, waits for them, and re-layouts  42.4 us (5%)
  between operations  15.5 us (2%)
  other arithmetic  9.67 us (1%)
  matrix products  9.33 us (1%)
    psum x1, waiting for transfers between devices, body(): summed_cols = lax.psum(partial_value, 'seq') + bias  200 us
    psum x1, waiting for transfers between devices, body(): lax.psum((local_weight * factor, local_acc * factor[..., None]), 'seq')  198 us
    unnamed x4, waiting for transfers between devices  108 us
    pmax x1, blocking collectives, body(): global_max = lax.pmax(local_max, 'seq')  91.2 us
    psum x1, blocking collectives, body(): lax.psum((local_weight * factor, local_acc * factor[..., None]), 'seq')  90 us
    psum x1, blocking collectives, body(): squares = lax.psum(jnp.sum(xf * xf, axis=2), 'seq')  54.7 us
    unnamed x46, local copies, waits for them, and re-layouts  28.4 us
  transfers between devices with their start and end apart: 4, of which 4 were waited for; matrix products, arithmetic and copies ran while one was open for 1% of the time, Pallas kernels for 0%

commit v1 on v0

--- a/solution.py
+++ b/solution.py
@@ -10,6 +10,10 @@
 KEY_COLUMNS = 1024
 epsilon = 1e-06
 masked_fill = -1e30
+
+
+def move_rails(field_in):
+    return lax.all_gather(field_in, "seq").sum(axis=0)
 
 
 def apply_rotary(values, token_positions):
@@ -55,7 +59,7 @@
     ).astype(jnp.bfloat16)
     partial_value = jnp.einsum("sbd,dc->sbc", normed, w_qkv, preferred_element_type=jnp.float32)
     bias = b_qkv.astype(jnp.float32)
-    summed_cols = lax.psum(partial_value, "seq") + bias
+    summed_cols = move_rails(partial_value) + bias
     combined_output = lax.all_to_all(summed_cols, "tensor", split_axis=1, concat_axis=2, tiled=True)
     token_positions = (
         (prefix_lens[0] + suffix_lens)[None, :]

time: 851 us -> 754 us (0.89)
  waiting for transfers between devices: 516 us -> 413 us
    psum x1 -> x0, waiting for transfers between devices: 200 us -> none  [body(): summed_cols = lax.psum(partial_value, 'seq') + bias]
    all_gather x0 -> x1, waiting for transfers between devices: none -> 98.5 us  [move_rails(): return lax.all_gather(field_in, 'seq').sum(axis=0)]
    unnamed x46 -> x49, local copies, waits for them, and re-layouts: 28.4 us -> 29.7 us
where the time goes in v1:
time: 754 us; the launch traced here: 753 us
  waiting for transfers between devices  413 us (55%)
  blocking collectives  249 us (33%)
  local copies, waits for them, and re-layouts  44.7 us (6%)
  between operations  15.5 us (2%)
  other arithmetic  14.5 us (2%)
  matrix products  9.21 us (1%)
  starting transfers between devices  7.57 us (1%)
    psum x1, waiting for transfers between devices, body(): lax.psum((local_weight * factor, local_acc * factor[..., None]), 'seq')  198 us
    unnamed x4, waiting for transfers between devices  107 us
    all_gather x1, waiting for transfers between devices, move_rails(): return lax.all_gather(field_in, 'seq').sum(axis=0)  98.5 us
    psum x1, blocking collectives, body(): lax.psum((local_weight * factor, local_acc * factor[..., None]), 'seq')  90 us
    pmax x1, blocking collectives, body(): global_max = lax.pmax(local_max, 'seq')  90 us
    psum x1, blocking collectives, body(): squares = lax.psum(jnp.sum(xf * xf, axis=2), 'seq')  54.7 us
    unnamed x49, local copies, waits for them, and re-layouts  29.7 us
  transfers between devices with their start and end apart: 4, of which 4 were waited for; matrix products, arithmetic and copies ran while one was open for 1% of the time, Pallas kernels for 0%

profile of v1, /device:TPU:2, one launch (start us, length us, event | category | flops | bytes accessed | tf_op | source)
XLA Modules:
  0.0 753.4 jit_solution(4849049653169618925)
XLA Ops:
  7.2 0.0 copy-start
  7.2 0.0 all-gather.3.cloned.1.call-start
  7.3 1.1 fusion.22
  8.4 54.7 %psum.21 = f32[4,64]{1,0:T(4,128)S(1)} all-reduce(f32[4,64]{1,0:T(4,128)S(1)} %fusion.22), channel_id=1, replica_groups=mesh['seq'=32,'tensor'=16] {'seq'}, use_global_device_ids=true, to_apply=%region_1.0 | all-reduce | flops 256 | bytes 2048 | tf_op jit(solution)/shard_map/psum | solution.py:56
  63.1 0.7 convert_element_type.43
  63.8 2.0 fusion.29
  65.8 0.0 all-gather.3.cloned.1.call-update
  66.5 0.0 copy-done.20
  66.5 0.1 add_convert_fusion.1
  66.6 0.1 multiply_cosine_fusion
  66.8 0.0 copy-start.11
  66.8 0.0 copy-start.13
  66.8 0.6 copy-done.11
  67.4 0.0 copy-done.13
  67.4 0.2 copy.204
  67.6 2.2 copy.205
  69.9 98.5 %all-gather.3.cloned.1.call-done = f32[128,64,448]{2,1,0:T(8,128)} async-done(((f32[4,64,448]{2,1,0:T(8,128)}), f32[128,64,448]{2,1,0:T(8,128)}) %all-gather.3.cloned.1.call-update) | async-done | bytes 14680080 | tf_op jit(solution)/shard_map/all_gather | solution.py:16
  168.3 7.8 %reduce_sum.46 = f32[4,64,448]{2,1,0:T(8,128)S(1)} reduce(f32[32,4,64,448]{3,2,1,0:T(8,128)} %bitcast.82, f32[]{:T(128)} %constant.9.clone.1), dimensions={0}, to_apply=%region_2.0 | reduce | flops 3555328 | bytes 15138820 | tf_op jit(solution)/shard_map/reduce_sum | solution.py:16
  176.1 0.1 broadcast_add_fusion
  176.2 1.1 copy.149
  177.3 7.3 all-to-all-start
  184.6 0.0 all-reduce.4.cloned.1.call-start
  184.7 0.6 iota_compare_fusion
  185.2 0.1 broadcast_compare_fusion
  185.3 9.9 %all-to-all-done = f32[4,64,448]{2,0,1:T(4,128)S(1)} async-done(((f32[4,64,448]{2,0,1:T(4,128)}), f32[4,64,448]{2,0,1:T(4,128)S(1)}, u32[]{:S(2)}, u32[]{:S(2)}) %all-to-all-start) | async-done | bytes 458784 | tf_op jit(solution)/shard_map/all_to_all | solution.py:63
  195.2 0.3 copy.150
  195.5 0.3 all_to_all.29
  195.9 0.3 subtract_convert_fusion
  196.2 0.2 maximum_bitcast_fusion
  196.5 0.7 fusion.53
  197.1 1.4 fusion.52
  198.6 0.6 copy.161
  199.2 90.0 %pmax.7 = f32[4,8,20]{2,1,0:T(8,128)} all-reduce(f32[4,8,20]{2,1,0:T(8,128)S(1)} %copy_maximum_fusion), channel_id=1, replica_groups=mesh['seq'=32,'tensor'=16] {'seq'}, use_global_device_ids=true, to_apply=%region_5.6 | all-reduce | flops 640 | bytes 5120 | tf_op jit(solution)/shard_map/pmax | solution.py:139
  289.2 0.6 slice_bitcast_fusion.1
  289.8 0.6 slice.42
  290.5 1.4 fusion.20
  291.9 1.1 fusion.12
  293.0 90.0 %psum.23 = f32[4,8,20]{2,1,0:T(8,128)S(1)} all-reduce(f32[4,8,20]{2,1,0:T(8,128)S(1)} %get-tuple-element.21), channel_id=1, replica_groups=mesh['seq'=32,'tensor'=16] {'seq'}, use_global_device_ids=true, to_apply=%region_10.11 | all-reduce | flops 640 | bytes 5120 | tf_op jit(solution)/shard_map/psum | solution.py:141
  383.1 0.1 fusion.51
  383.2 0.0 copy-start.1
  383.2 1.2 convolution_bitcast_fusion
  384.5 1.2 fusion.4
  385.6 0.0 all-reduce.4.cloned.1.call-update
  385.7 0.2 all-reduce.6.cloned.1.call-start
  385.9 0.1 multiply_subtract_fusion
  386.0 0.3 fusion.54
  386.3 0.1 fusion.37
  386.5 197.8 %all-reduce.4.cloned.1.call-done = f32[4,8,20,128]{3,2,0,1:T(8,128)} async-done(((f32[4,8,20,128]{3,2,0,1:T(8,128)}), f32[4,8,20,128]{3,2,0,1:T(8,128)}) %all-reduce.4.cloned.1.call-update) | async-done | bytes 327696 | tf_op jit(solution)/shard_map/psum | solution.py:141
  584.3 1.5 fusion.6
  585.8 0.1 copy.175
  585.9 4.5 copy.195
  590.4 11.0 %reshape.166 = bf16[16,2,2560]{2,1,0:T(2,128)(2,1)S(1)} reshape(bf16[5120,4,4]{2,1,0:T(4,128)(2,1)} %bitcast.80) | data formatting | bytes 327680
  601.3 13.9 %all_to_all.36 = bf16[16,2,2560]{2,1,0:T(2,128)(2,1)S(1)} all-to-all(bf16[16,2,2560]{2,1,0:T(2,128)(2,1)S(1)} %reshape.166), channel_id=1, replica_groups=mesh['seq'=32,'tensor'=16] {'tensor'}, dimensions={0} | all-to-all | bytes 327680 | tf_op jit(solution)/shard_map/all_to_all | solution.py:176
  615.2 12.3 %reshape.167 = bf16[5120,4,4]{2,1,0:T(4,128)(2,1)} reshape(bf16[16,2,2560]{2,1,0:T(2,128)(2,1)S(1)} %all_to_all.36) | data formatting | bytes 327680
  627.5 6.4 copy.196
  634.0 0.1 copy.179
  634.1 0.1 all_to_all.33
  634.2 0.9 fusion.34
  635.1 0.0 all-reduce.6.cloned.1.call-update
  635.1 1.3 dynamic-slice
  637.1 0.7 copy.180
  637.7 0.7 fusion.46
  638.5 107.0 %all-reduce.6.cloned.1.call-done = f32[4,64,160]{2,1,0:T(8,128)} async-done(((f32[4,64,160]{2,1,0:T(8,128)}), f32[4,64,160]{2,1,0:T(8,128)}) %all-reduce.6.cloned.1.call-update) | async-done | bytes 163856
  745.5 1.4 constant_dynamic-slice_fusion
  (55 shorter events, 0.3 us)
Async XLA Ops:
  7.2 190.0 %copy-start = (bf16[4,128,1024]{2,1,0:T(8,128)(2,1)S(1)}, bf16[4,128,1024]{2,1,0:T(8,128)(2,1)}, u32[]{:S(2)}) copy-start(bf16[4,128,1024]{2,1,0:T(8,128)(2,1)} %param.18) | copy-start | bytes 3145732
  7.2 59.3 %copy-start.20 = (s32[4]{0:T(128)S(1)}, s32[4]{0:T(128)}, u32[]{:S(2)}) copy-start(s32[4]{0:T(128)} %param.21) | copy-start | bytes 52
  7.2 60.2 %copy-start.17 = (bf16[448]{0:T(512)(128)(2,1)S(1)}, bf16[448]{0:T(512)(128)(2,1)}, u32[]{:S(2)}) copy-start(bf16[448]{0:T(512)(128)(2,1)} %param.14) | copy-start | bytes 2692
  7.2 60.2 %copy-start.4 = (bf16[1,384,1024]{2,1,0:T(8,128)(2,1)S(1)}, bf16[1,384,1024]{2,1,0:T(8,128)(2,1)}, u32[]{:S(2)}) copy-start(bf16[1,384,1024]{2,1,0:T(8,128)(2,1)} %param.16) | copy-start | bytes 2359300
  7.2 161.1 %all-gather.3.cloned.1.call-start = ((), (), s32[]{:S(2)}) async-start(), calls=%async_computation.3 | async-start | bytes 17301504 | tf_op jit(solution)/shard_map/all_gather | solution.py:16
  66.8 0.6 copy-start.11
  66.8 0.6 copy-start.13
  69.9 126.6 %copy-start.16 = (pred[384]{0:T(512)(128)(4,1)}, pred[384]{0:T(512)(128)(4,1)S(1)}, u32[]{:S(2)}) copy-start(pred[384]{0:T(512)(128)(4,1)S(1)} %add_compare_fusion) | copy-start | bytes 1156
  177.3 17.9 %all-to-all-start = ((f32[4,64,448]{2,0,1:T(4,128)}), f32[4,64,448]{2,0,1:T(4,128)S(1)}, u32[]{:S(2)}, u32[]{:S(2)}) async-start(f32[4,64,448]{2,0,1:T(4,128)} %copy.149), calls=%async_computation | async-start | bytes 1048576 | tf_op jit(solution)/shard_map/all_to_all | solution.py:63
  184.6 399.7 %all-reduce.4.cloned.1.call-start = ((), (), s32[]{:S(2)}) async-start(), calls=%async_computation.2 | async-start | bytes 786432 | tf_op jit(solution)/shard_map/psum | solution.py:141
  185.3 11.8 %copy-start.19 = (pred[4,128]{1,0:T(4,128)(4,1)}, pred[4,128]{1,0:T(4,128)(4,1)S(1)}, u32[]{:S(2)}) copy-start(pred[4,128]{1,0:T(4,128)(4,1)S(1)} %broadcast_compare_fusion) | copy-start | bytes 1540
  196.4 2.1 copy-start.2
  289.2 3.8 copy-start.7
  290.4 92.6 %copy-start.6 = (f32[4,4,1024]{2,1,0:T(4,128)S(1)}, f32[4,4,1024]{2,1,0:T(4,128)}, u32[]{:S(2)}) copy-start(f32[4,4,1024]{2,1,0:T(4,128)} %get-tuple-element.24) | copy-start | bytes 196612
  290.4 92.7 %copy-start.5 = (bf16[48,8,8,128]{3,2,1,0:T(8,128)(2,1)S(1)}, bf16[48,8,8,128]{3,2,1,0:T(8,128)(2,1)}, u32[]{:S(2)}) copy-start(bf16[48,8,8,128]{3,2,1,0:T(8,128)(2,1)} %copy.205) | copy-start | bytes 2359300
  290.5 92.7 %copy-start.15 = (f32[4,8,20]{2,0,1:T(4,128)S(1)}, f32[4,8,20]{2,0,1:T(4,128)}, u32[]{:S(2)}) copy-start(f32[4,8,20]{2,0,1:T(4,128)} %copy.161) | copy-start | bytes 7684
  383.2 1.3 copy-start.1
  384.4 1.5 copy-start.12
  384.4 1.5 copy-start.14
  384.5 1.6 copy-start.3
  384.5 1.6 copy-start.18
  384.5 1.9 copy-start.8
  385.6 0.8 copy-start.9
  385.7 359.8 %all-reduce.6.cloned.1.call-start = ((), (), s32[]{:S(2)}) async-start(), calls=%async_computation.4 | async-start | bytes 524288
  627.5 6.6 copy-start.10
Sparse Core Ops, SparseCore 0:
  66.0 102.3 all-gather.2
  385.8 198.4 all-reduce.3
  635.3 110.1 all-reduce.5
